TPU v7x, 256 devices: a whole 4x4x8 slice. The times are simulated.
256 devices in a mesh: tm: 8 (over y, core), node: 32 (over z, x).
Axes of the slice: x: 4, y: 4, z: 8, core: 2. Of those that a mesh axis runs over, the one named last changes fastest.
Arguments:
- inputs: bfloat16 [32768, 2048], P('node', 'tm'), may hold values from -6 to 6
- conv_weight: bfloat16 [3, 64, 256], replicated, may hold values from -0.4375 to 0.4375
- conv_bias: float32 [256], replicated, may hold values from -3 to 3
- tile_values: bfloat16 [256, 4, 128, 128], P('node'), may hold values from -0.25 to 0.25
- tile_cols: int32 [256, 4], P('node'), may hold values from -2 to 257, as said below
- tile_count: int32 [256], P('node'), may hold values from 1 to 4, as said below
- cheb_weight: bfloat16 [3, 128, 128], replicated, may hold values from -0.3125 to 0.3125
- cheb_bias: float32 [128], replicated, may hold values from -3 to 3
Outputs:
- graph_out: bfloat16 [32768, 32, 128], P('node', 'tm')
Inputs may be any that keep to these rules, and one draw needn't show every extreme that they name: `tile_cols`: tile 0 of block b names b itself; tiles 1 to 3 name b plus distinct nonzero offsets in -2 to 2. Tile slots at or after tile_count[b] are unused.
All inputs are finite; a program needn't handle non-finite values.
Results may differ from a plain program's by a relative error of at most 0.0056.
Values may be sent and summed in bfloat16 or wider, within the bound.
No kernel may reach another device: no remote copies, remote signals or barrier semaphores. Data moves between devices by JAX's collectives and lax.ppermute only.
A program may use at most 64 MiB of HBM per device.

v0:
```python
import jax
import jax.numpy as jnp
from jax import lax
from jax.sharding import PartitionSpec as P

HB = 2
TPB = 4


def passed_along(value, axis, by):
    length = lax.axis_size(axis)
    pairs = [(i, i + by) for i in range(length) if 0 <= i + by < length]
    return lax.ppermute(value, axis, pairs)


def build_band(tile_set, col_ids, live_count, first_block):
    block_count = tile_set.shape[0]
    row_ids = first_block + jnp.arange(block_count, dtype=jnp.int32)
    offset = col_ids - row_ids[:, None] + HB
    live_mask = jnp.arange(TPB, dtype=jnp.int32)[None, :] < live_count[:, None]
    tiles = tile_set.astype(jnp.float32)
    bands = []
    for o in range(2 * HB + 1):
        pick = ((offset == o) & live_mask).astype(jnp.float32)
        bands.append(jnp.sum(pick[:, :, None, None] * tiles, axis=1).astype(jnp.bfloat16))
    return bands


def band_product(bands, extended):
    block_count = bands[0].shape[0]
    total = None
    for offset in range(2 * HB + 1):
        term = jnp.einsum(
            "bpq,bqf->bpf",
            bands[offset],
            extended[offset : offset + block_count],
            preferred_element_type=jnp.float32,
        )
        total = term if total is None else total + term
    return total


def pair_weight(conv_weight):
    taps, chan_in, width = conv_weight.shape
    eye = jnp.eye(2, dtype=conv_weight.dtype)
    blocks = [jnp.kron(eye, conv_weight[k]) for k in range(taps)]
    rows_in = jnp.arange(2 * chan_in, dtype=jnp.int32)[:, None]
    cols_out = jnp.arange(2 * width, dtype=jnp.int32)[None, :]
    place = (cols_out == rows_in // chan_in * width + rows_in % chan_in).astype(conv_weight.dtype)
    return jnp.concatenate(blocks + [place], axis=0)


def block_diag(weight, steps):
    return jnp.kron(jnp.eye(steps, dtype=weight.dtype), weight)


def stage(
    inputs, conv_weight, conv_bias, tile_values, tile_cols, tile_count, cheb_weight, cheb_bias
):
    row_count, flat_width = inputs.shape
    chan_in = conv_weight.shape[1]
    chan_out = cheb_weight.shape[2]
    steps_dev = flat_width // chan_in
    block_count, block_rows = (tile_values.shape[0], tile_values.shape[2])
    feat_width = steps_dev * chan_out
    earlier = passed_along(inputs, "tm", 1)
    wpair = pair_weight(conv_weight)
    pair_w = 2 * chan_in
    pieces = []
    for p in range(steps_dev // 2):
        w_new, w_mid, w_old, w_place = (wpair[i * pair_w : (i + 1) * pair_w] for i in range(4))
        newest = inputs[:, p * pair_w : (p + 1) * pair_w]
        cur_l = [newest, newest]
        cur_w = [w_new, w_place]
        prev_l = []
        prev_w = []
        for lag, w in ((1, w_mid), (2, w_old)):
            q = p - lag
            if q >= 0:
                cur_l.append(inputs[:, q * pair_w : (q + 1) * pair_w])
                cur_w.append(w)
            else:
                q += steps_dev // 2
                prev_l.append(earlier[:, q * pair_w : (q + 1) * pair_w])
                prev_w.append(w)
        mixed = jnp.dot(
            jnp.concatenate(cur_l, axis=1), jnp.concatenate(cur_w, axis=0), preferred_element_type=jnp.float32
        )
        mixed = mixed + jnp.dot(
            jnp.concatenate(prev_l, axis=1), jnp.concatenate(prev_w, axis=0), preferred_element_type=jnp.float32
        )
        for tt in range(2):
            lo = tt * 2 * chan_out
            linear = mixed[:, lo : lo + chan_out] + conv_bias[:chan_out]
            gate = mixed[:, lo + chan_out : lo + 2 * chan_out] + conv_bias[chan_out:]
            pieces.append(linear * jax.nn.sigmoid(gate))
    flat_features = jnp.concatenate(pieces, axis=1).astype(jnp.bfloat16)
    first_block = lax.axis_index("node") * block_count
    band_tiles = build_band(tile_values, tile_cols, tile_count, first_block)
    node_count = lax.axis_size("node")
    to_right = [(i, i + 1) for i in range(node_count - 1)]
    to_left = [(i + 1, i) for i in range(node_count - 1)]
    rim = HB * block_rows
    edge_ids = list(range(HB)) + list(range(block_count - HB, block_count))
    halo_band = []
    for b in edge_ids:
        terms = []
        for o in range(2 * HB + 1):
            j = b + o
            if j < HB or j >= block_count + HB:
                terms.append(band_tiles[o][b])
        while len(terms) < HB:
            terms.append(jnp.zeros_like(band_tiles[0][0]))
        halo_band.append(jnp.stack(terms))
    halo_band = jnp.stack(halo_band)

    def halo_blocks(left, right):
        lb = left.reshape(HB, block_rows, feat_width)
        rb = right.reshape(HB, block_rows, feat_width)
        picks = []
        for b in edge_ids:
            terms = []
            for o in range(2 * HB + 1):
                j = b + o
                if j < HB:
                    terms.append(lb[j])
                elif j >= block_count + HB:
                    terms.append(rb[j - block_count - HB])
            while len(terms) < HB:
                terms.append(terms[-1])
            picks.append(jnp.stack(terms))
        return jnp.stack(picks)

    def halo_part(left, right):
        part = jnp.einsum(
            "bkpq,bkqf->bpf", halo_band, halo_blocks(left, right), preferred_element_type=jnp.float32
        )
        middle = jnp.zeros((block_count - 2 * HB, block_rows, feat_width), jnp.float32)
        return jnp.concatenate([part[:HB], middle, part[HB:]], axis=0)

    def own_part(values):
        padded = jnp.pad(values.reshape(block_count, block_rows, feat_width), ((HB, HB), (0, 0), (0, 0)))
        return band_product(band_tiles, padded)

    feat_left = lax.ppermute(flat_features[row_count - rim :], "node", to_right)
    feat_right = lax.ppermute(flat_features[:rim], "node", to_left)
    one_own = own_part(flat_features)
    order_one = (one_own + halo_part(feat_left, feat_right)).astype(jnp.bfloat16)
    order_one = order_one.reshape(row_count, feat_width)
    one_left = lax.ppermute(order_one[row_count - rim :], "node", to_right)
    one_right = lax.ppermute(order_one[:rim], "node", to_left)
    two_own = own_part(order_one)
    kron = [block_diag(cheb_weight[k], steps_dev) for k in range(3)]
    early = jnp.dot(
        jnp.concatenate([flat_features, order_one], axis=1),
        jnp.concatenate(kron[:2], axis=0),
        preferred_element_type=jnp.float32,
    ) + jnp.tile(cheb_bias, steps_dev)
    order_two = (two_own + halo_part(one_left, one_right)).reshape(row_count, feat_width)
    cheb_two = (2.0 * order_two - flat_features.astype(jnp.float32)).astype(jnp.bfloat16)
    result = early + jnp.dot(cheb_two, kron[2], preferred_element_type=jnp.float32)
    return jax.nn.relu(result).astype(jnp.bfloat16).reshape(row_count, steps_dev, chan_out)


def solution(mesh):
    placed = (
        P("node", "tm"),
        P(),
        P(),
        P("node", None, None, None),
        P("node", None),
        P("node"),
        P(),
        P(),
    )
    return jax.shard_map(stage, mesh=mesh, in_specs=placed, out_specs=P("node", "tm", None), check_vma=False)
```

profile of v0, /device:TPU:128, one launch (start us, length us, event | category | flops | bytes accessed | tf_op | source)
XLA Modules:
  0.0 52.2 jit_solution(1832840132477430070)
XLA Ops:
  0.0 1.9 %collective-permute-start = (bf16[1024,256]{1,0:T(8,128)(2,1)}, bf16[1024,256]{1,0:T(8,128)(2,1)S(1)}, u32[]{:S(2)}, u32[]{:S(2)}) collective-permute-start(bf16[1024,256]{1,0:T(8,128)(2,1)} %param.8), channel_id=1, source_target_pairs={{0,32},{32,64},{64,96},{96,128},{128,160},{160,192},{192,224},{1,3... | collective-permute-start | bytes 1572872 | tf_op jit(solution)/shard_map/ppermute | solution.py:13
  1.9 1.1 %fusion.131 = (bf16[1024,128]{1,0:T(8,128)(2,1)S(1)}, bf16[1024,128]{1,0:T(8,128)(2,1)S(1)}) fusion(bf16[1024,256]{1,0:T(8,128)(2,1)} %param.8), kind=kLoop, calls=%fused_computation.212 | loop fusion | bytes 1048576 | tf_op jit(solution)/shard_map/slice | solution.py:72
  3.0 0.8 %fusion.135 = (f32[128]{0:T(128)S(1)}, f32[128]{0:T(128)S(1)}) fusion(f32[256]{0:T(256)} %param.10), kind=kLoop, calls=%fused_computation.216 | loop fusion | bytes 2048 | tf_op jit(solution)/shard_map/slice | solution.py:94
  3.9 0.8 %slice_bitcast_fusion.12 = (bf16[64,256]{1,0:T(8,128)(2,1)S(1)}, bf16[64,256]{1,0:T(8,128)(2,1)S(1)}, bf16[64,256]{1,0:T(8,128)(2,1)S(1)}) fusion(bf16[3,64,256]{2,1,0:T(8,128)(2,1)} %param.9), kind=kLoop, calls=%fused_computation.163 | loop fusion | bytes 196608 | tf_op jit(solution)/shard_map/jit(kron)/mul | solution.py:46
  5.6 1.2 %fusion.2 = (bf16[8,128,128]{2,1,0:T(8,128)(2,1)S(1)}, bf16[8,128,128]{2,1,0:T(8,128)(2,1)S(1)}, bf16[8,128,128]{2,1,0:T(8,128)(2,1)S(1)}, bf16[8,128,128]{2,1,0:T(8,128)(2,1)S(1)}, bf16[8,128,128]{2,1,0:T(8,128)(2,1)S(1)}) fusion(bf16[8,4,128,128]{3,2,1,0:T(8,128)(2,1)S(1)} %copy-done.1, f32[8,4]{1,0:T(8,128)S(1)} %copy.12, f32[8,4]{1,0:T(8,128)S(1)} %copy.11, ...), kind=kLoop, calls=%fused_computation.7 | loop fusion | flops 5111808 | bytes 2359936 | tf_op jit(solution)/shard_map/reduce_sum | solution.py:25
  6.9 0.4 fusion.61
  7.3 0.7 %fusion.33 = f32[1024,512]{1,0:T(8,128)S(1)} fusion(bf16[1024,128]{1,0:T(8,128)(2,1)S(1)} %get-tuple-element.27, bf16[1024,128]{1,0:T(8,128)(2,1)S(1)} %get-tuple-element.26, bf16[128,512]{1,0:T(8,128)(2,1)S(1)} %bitcast.127, bf16[128,512]{1,0:T(8,128)(2,1)S(1)} %fusion.91, bf16[128,512]{1,0:T(8,128)(2,1)S(1)} %bitcast.130), kind=kOutput, calls=%fused_computation.54 | convolution fusion | flops 406192128 | bytes 3014656 | tf_op jit(solution)/shard_map/dot_general | solution.py:86
  8.2 0.7 %broadcast_multiply_fusion = (bf16[4,128,4,128]{3,2,1,0:T(4,128)(2,1)S(1)}, bf16[4,128,4,128]{3,2,1,0:T(4,128)(2,1)S(1)}, bf16[4,128,4,128]{3,2,1,0:T(4,128)(2,1)S(1)}) fusion(bf16[128,128]{1,0:T(8,128)(2,1)S(1)} %get-tuple-element.50, bf16[4,4]{1,0:T(4,128)(2,1)S(1)} %fusion.106, bf16[128,128]{1,0:T(8,128)(2,1)S(1)} %get-tuple-element.52, ...), kind=kLoop, calls=%fused_computation.135 | loop fusion | flops 786432 | bytes 1671200 | tf_op jit(solution)/shard_map/jit(kron)/mul | solution.py:54
  9.1 0.4 convolution_add_fusion
  12.1 4.2 %collective-permute-start.2 = (bf16[256,512]{1,0:T(8,128)(2,1)S(1)}, bf16[256,512]{1,0:T(8,128)(2,1)S(1)}, u32[]{:S(2)}, u32[]{:S(2)}) collective-permute-start(bf16[256,512]{1,0:T(8,128)(2,1)S(1)} %get-tuple-element.25), channel_id=1, source_target_pairs={{1,0},{2,1},{3,2},{4,3},{5,4},{6,5},{7,6},{8,7},{9,8},{10,9},{11,1... | collective-permute-start | bytes 786440 | tf_op jit(solution)/shard_map/ppermute | solution.py:146
  16.3 1.9 %collective-permute-start.1 = (bf16[256,512]{1,0:T(8,128)(2,1)S(1)}, bf16[256,512]{1,0:T(8,128)(2,1)S(1)}, u32[]{:S(2)}, u32[]{:S(2)}) collective-permute-start(bf16[256,512]{1,0:T(8,128)(2,1)S(1)} %get-tuple-element.24), channel_id=1, source_target_pairs={{0,1},{1,2},{2,3},{3,4},{4,5},{5,6},{6,7},{7,8},{8,9},{9,10},{10,1... | collective-permute-start | bytes 786440 | tf_op jit(solution)/shard_map/ppermute | solution.py:145
  18.2 0.4 fusion.94
  18.7 3.7 %collective-permute-done.2 = bf16[256,512]{1,0:T(8,128)(2,1)S(1)} collective-permute-done((bf16[256,512]{1,0:T(8,128)(2,1)S(1)}, bf16[256,512]{1,0:T(8,128)(2,1)S(1)}, u32[]{:S(2)}, u32[]{:S(2)}) %collective-permute-start.2) | collective-permute-done | bytes 262176 | tf_op jit(solution)/shard_map/ppermute | solution.py:146
  22.3 7.8 %collective-permute-done.1 = bf16[256,512]{1,0:T(8,128)(2,1)S(1)} collective-permute-done((bf16[256,512]{1,0:T(8,128)(2,1)S(1)}, bf16[256,512]{1,0:T(8,128)(2,1)S(1)}, u32[]{:S(2)}, u32[]{:S(2)}) %collective-permute-start.1) | collective-permute-done | bytes 262176 | tf_op jit(solution)/shard_map/ppermute | solution.py:145
  30.7 0.6 %fusion.5 = bf16[8,128,512]{2,1,0:T(8,128)(2,1)S(1)} fusion(f32[2,128,512]{2,1,0:T(8,128)S(1)} %get-tuple-element.23, f32[2,128,512]{2,1,0:T(8,128)S(1)} %get-tuple-element.22, f32[8,128,512]{2,1,0:T(8,128)S(1)} %fusion.11, f32[8,128,512]{2,1,0:T(8,128)S(1)} %fusion.94, f32[8,128,512]{2,1,0:T(8,128)S(1)} %fusion.9, f32[8,128,512]{2,1,0:T(8,128)S(1)} %fusion.10, ...), kind=kOutput, calls=%fused_computation.11 | convolution fusion | flops 138412032 | bytes 11796512 | tf_op jit(solution)/shard_map/bpq,bqf->bpf/dot_general | solution.py:33
  31.7 0.4 fusion.136
  32.5 1.9 %collective-permute-start.4 = (bf16[256,512]{1,0:T(8,128)(2,1)S(1)}, bf16[256,512]{1,0:T(8,128)(2,1)S(1)}, u32[]{:S(2)}, u32[]{:S(2)}) collective-permute-start(bf16[256,512]{1,0:T(8,128)(2,1)S(1)} %bitcast.135), channel_id=1, source_target_pairs={{1,0},{2,1},{3,2},{4,3},{5,4},{6,5},{7,6},{8,7},{9,8},{10,9},{11,1... | collective-permute-start | bytes 786440 | tf_op jit(solution)/shard_map/ppermute | solution.py:151
  34.5 4.1 %collective-permute-start.3 = (bf16[256,512]{1,0:T(8,128)(2,1)S(1)}, bf16[256,512]{1,0:T(8,128)(2,1)S(1)}, u32[]{:S(2)}, u32[]{:S(2)}) collective-permute-start(bf16[256,512]{1,0:T(8,128)(2,1)S(1)} %bitcast.134), channel_id=1, source_target_pairs={{0,1},{1,2},{2,3},{3,4},{4,5},{5,6},{6,7},{7,8},{8,9},{9,10},{10,1... | collective-permute-start | bytes 786440 | tf_op jit(solution)/shard_map/ppermute | solution.py:150
  38.7 1.3 %fusion.22 = f32[1024,512]{0,1:T(8,128)S(1)} fusion(bf16[1024,1024]{1,0:T(8,128)(2,1)S(1)} %constant_dynamic-update-slice_fusion, bf16[512,512]{1,0:T(8,128)(2,1)S(1)} %get-tuple-element.73, bf16[512,512]{1,0:T(8,128)(2,1)S(1)} %get-tuple-element.74), kind=kOutput, calls=%fused_computation.43 | convolution fusion | flops 1075838976 | bytes 5242880 | tf_op jit(solution)/shard_map/dot_general | solution.py:154
  40.5 2.6 %collective-permute-done.4 = bf16[256,512]{1,0:T(8,128)(2,1)S(1)} collective-permute-done((bf16[256,512]{1,0:T(8,128)(2,1)S(1)}, bf16[256,512]{1,0:T(8,128)(2,1)S(1)}, u32[]{:S(2)}, u32[]{:S(2)}) %collective-permute-start.4) | collective-permute-done | bytes 262176 | tf_op jit(solution)/shard_map/ppermute | solution.py:151
  43.1 5.2 %collective-permute-done.3 = bf16[256,512]{1,0:T(8,128)(2,1)S(1)} collective-permute-done((bf16[256,512]{1,0:T(8,128)(2,1)S(1)}, bf16[256,512]{1,0:T(8,128)(2,1)S(1)}, u32[]{:S(2)}, u32[]{:S(2)}) %collective-permute-start.3) | collective-permute-done | bytes 262176 | tf_op jit(solution)/shard_map/ppermute | solution.py:150
  48.8 1.1 %fusion.8 = bf16[8,128,512]{2,1,0:T(8,128)(2,1)S(1)} fusion(f32[2,128,512]{2,1,0:T(8,128)S(1)} %get-tuple-element.19, f32[2,128,512]{2,1,0:T(8,128)S(1)} %get-tuple-element.18, f32[8,128,512]{2,1,0:T(8,128)S(1)} %fusion.14, f32[8,128,512]{2,1,0:T(8,128)S(1)} %fusion.136, f32[8,128,512]{2,1,0:T(8,128)S(1)} %fusion.12, f32[8,128,512]{2,1,0:T(8,128)S(1)} %fusion.13, ...), kind=kOutput, calls=%fused_computation.15 | convolution fusion | flops 143654912 | bytes 12845088 | tf_op jit(solution)/shard_map/bpq,bqf->bpf/dot_general | solution.py:33
  50.0 0.8 %maximum_convert_fusion = bf16[1024,512]{0,1:T(8,128)(2,1)S(1)} fusion(f32[1024,512]{0,1:T(8,128)S(1)} %fusion.22, bf16[1024,512]{1,0:T(8,128)(2,1)S(1)} %bitcast.124, f32[512]{0:T(512)S(1)} %broadcast_bitcast_fusion, bf16[64,8,4,128]{3,2,1,0:T(4,128)(2,1)S(1)} %bitcast.126), kind=kOutput, calls=%fused_computation.17 | convolution fusion | flops 538968064 | bytes 4720640 | tf_op jit(solution)/shard_map/dot_general | solution.py:161
  50.7 1.4 %copy.15 = bf16[1024,4,128]{2,1,0:T(4,128)(2,1)} copy(bf16[1024,4,128]{0,2,1:T(8,128)(2,1)S(1)} %bitcast.125) | data formatting | bytes 2097152 | tf_op jit(solution)/shard_map/reshape | solution.py:162
  (65 shorter events, 6.3 us)
Async XLA Ops:
  0.0 6.9 %copy-start = (f32[128]{0:T(128)S(1)}, f32[128]{0:T(128)}, u32[]{:S(2)}) copy-start(f32[128]{0:T(128)} %param.15) | copy-start | bytes 1540
  0.0 5.2 %copy-start.4 = (s32[8]{0:T(128)S(1)}, s32[8]{0:T(128)}, u32[]{:S(2)}) copy-start(s32[8]{0:T(128)} %param.13) | copy-start | bytes 100
  0.0 5.2 %copy-start.3 = (s32[8,4]{0,1:T(4,128)S(1)}, s32[8,4]{0,1:T(4,128)}, u32[]{:S(2)}) copy-start(s32[8,4]{0,1:T(4,128)} %param.12) | copy-start | bytes 388
  0.0 5.6 %copy-start.1 = (bf16[8,4,128,128]{3,2,1,0:T(8,128)(2,1)S(1)}, bf16[8,4,128,128]{3,2,1,0:T(8,128)(2,1)}, u32[]{:S(2)}) copy-start(bf16[8,4,128,128]{3,2,1,0:T(8,128)(2,1)} %param.11) | copy-start | bytes 3145732
  0.0 9.0 %collective-permute-start = (bf16[1024,256]{1,0:T(8,128)(2,1)}, bf16[1024,256]{1,0:T(8,128)(2,1)S(1)}, u32[]{:S(2)}, u32[]{:S(2)}) collective-permute-start(bf16[1024,256]{1,0:T(8,128)(2,1)} %param.8), channel_id=1, source_target_pairs={{0,32},{32,64},{64,96},{96,128},{128,160},{160,192},{192,224},{1,3... | collective-permute-start | bytes 1572872 | tf_op jit(solution)/shard_map/ppermute | solution.py:13
  4.7 2.2 %copy-start.2 = (bf16[3,128,128]{2,1,0:T(8,128)(2,1)S(1)}, bf16[3,128,128]{2,1,0:T(8,128)(2,1)}, u32[]{:S(2)}) copy-start(bf16[3,128,128]{2,1,0:T(8,128)(2,1)} %param.14) | copy-start | bytes 294916
  12.1 10.2 %collective-permute-start.2 = (bf16[256,512]{1,0:T(8,128)(2,1)S(1)}, bf16[256,512]{1,0:T(8,128)(2,1)S(1)}, u32[]{:S(2)}, u32[]{:S(2)}) collective-permute-start(bf16[256,512]{1,0:T(8,128)(2,1)S(1)} %get-tuple-element.25), channel_id=1, source_target_pairs={{1,0},{2,1},{3,2},{4,3},{5,4},{6,5},{7,6},{8,7},{9,8},{10,9},{11,1... | collective-permute-start | bytes 786440 | tf_op jit(solution)/shard_map/ppermute | solution.py:146
  16.3 13.8 %collective-permute-start.1 = (bf16[256,512]{1,0:T(8,128)(2,1)S(1)}, bf16[256,512]{1,0:T(8,128)(2,1)S(1)}, u32[]{:S(2)}, u32[]{:S(2)}) collective-permute-start(bf16[256,512]{1,0:T(8,128)(2,1)S(1)} %get-tuple-element.24), channel_id=1, source_target_pairs={{0,1},{1,2},{2,3},{3,4},{4,5},{5,6},{6,7},{7,8},{8,9},{9,10},{10,1... | collective-permute-start | bytes 786440 | tf_op jit(solution)/shard_map/ppermute | solution.py:145
  32.5 10.5 %collective-permute-start.4 = (bf16[256,512]{1,0:T(8,128)(2,1)S(1)}, bf16[256,512]{1,0:T(8,128)(2,1)S(1)}, u32[]{:S(2)}, u32[]{:S(2)}) collective-permute-start(bf16[256,512]{1,0:T(8,128)(2,1)S(1)} %bitcast.135), channel_id=1, source_target_pairs={{1,0},{2,1},{3,2},{4,3},{5,4},{6,5},{7,6},{8,7},{9,8},{10,9},{11,1... | collective-permute-start | bytes 786440 | tf_op jit(solution)/shard_map/ppermute | solution.py:151
  34.5 13.8 %collective-permute-start.3 = (bf16[256,512]{1,0:T(8,128)(2,1)S(1)}, bf16[256,512]{1,0:T(8,128)(2,1)S(1)}, u32[]{:S(2)}, u32[]{:S(2)}) collective-permute-start(bf16[256,512]{1,0:T(8,128)(2,1)S(1)} %bitcast.134), channel_id=1, source_target_pairs={{0,1},{1,2},{2,3},{3,4},{4,5},{5,6},{6,7},{7,8},{8,9},{9,10},{10,1... | collective-permute-start | bytes 786440 | tf_op jit(solution)/shard_map/ppermute | solution.py:150
where the time goes:
time: 52.5 us; the launch traced here: 52.2 us
  waiting for transfers between devices  19.2 us (37%)
  starting transfers between devices  14.1 us (27%)
  matrix products  9.76 us (19%)
  local copies, waits for them, and re-layouts  5.24 us (10%)
  other arithmetic  3.44 us (7%)
    ppermute x1, waiting for transfers between devices, stage(): feat_left = lax.ppermute(flat_features[row_count - rim:], 'node', to_right)  7.78 us
    ppermute x1, waiting for transfers between devices, stage(): one_left = lax.ppermute(order_one[row_count - rim:], 'node', to_right)  5.18 us
    dot_general x10, matrix products, band_product(): jnp.einsum('bpq,bqf->bpf', bands[offset], extended[offset:offset + block_...  4.95 us
    ppermute x1, starting transfers between devices, stage(): feat_right = lax.ppermute(flat_features[:rim], 'node', to_left)  4.21 us
    ppermute x1, starting transfers between devices, stage(): one_left = lax.ppermute(order_one[row_count - rim:], 'node', to_right)  4.1 us
    ppermute x1, waiting for transfers between devices, stage(): feat_right = lax.ppermute(flat_features[:rim], 'node', to_left)  3.65 us
    ppermute x1, waiting for transfers between devices, stage(): one_right = lax.ppermute(order_one[:rim], 'node', to_left)  2.59 us
    ppermute x1, starting transfers between devices, stage(): feat_left = lax.ppermute(flat_features[row_count - rim:], 'node', to_right)  1.92 us
  transfers between devices with their start and end apart: 5, of which 4 were waited for; matrix products, arithmetic and copies ran while one was open for 18% of the time, Pallas kernels for 0%

commit v1 on v0

--- a/solution.py
+++ b/solution.py
@@ -65,6 +65,7 @@
     feat_width = steps_dev * chan_out
     earlier = passed_along(inputs, "tm", 1)
     wpair = pair_weight(conv_weight)
+    bias_row = jnp.tile(conv_bias, 2)[None, :]
     pair_w = 2 * chan_in
     pieces = []
     for p in range(steps_dev // 2):
@@ -89,10 +90,11 @@
         mixed = mixed + jnp.dot(
             jnp.concatenate(prev_l, axis=1), jnp.concatenate(prev_w, axis=0), preferred_element_type=jnp.float32
         )
+        mixed = mixed + bias_row
         for tt in range(2):
             lo = tt * 2 * chan_out
-            linear = mixed[:, lo : lo + chan_out] + conv_bias[:chan_out]
-            gate = mixed[:, lo + chan_out : lo + 2 * chan_out] + conv_bias[chan_out:]
+            linear = mixed[:, lo : lo + chan_out]
+            gate = mixed[:, lo + chan_out : lo + 2 * chan_out]
             pieces.append(linear * jax.nn.sigmoid(gate))
     flat_features = jnp.concatenate(pieces, axis=1).astype(jnp.bfloat16)
     first_block = lax.axis_index("node") * block_count

time: 52.5 us -> 51.7 us (0.985)
  local copies, waits for them, and re-layouts: 5.24 us -> 4.49 us
    slice x1 -> x0, local copies, waits for them, and re-layouts: 0.76 us -> none  [stage(): linear = mixed[:, lo:lo + chan_out] + conv_bias[:chan_out]]
  transfers between devices with their start and end apart: 5 -> 5, of which waited for: 4 -> 4; matrix products, arithmetic and copies ran while one was open for 18% -> 16% of each run, Pallas kernels for 0% -> 0%
where the time goes in v1:
time: 51.7 us; the launch traced here: 51.4 us
  waiting for transfers between devices  19.2 us (37%)
  starting transfers between devices  14 us (27%)
  matrix products  9.77 us (19%)
  local copies, waits for them, and re-layouts  4.49 us (9%)
  other arithmetic  3.43 us (7%)
    ppermute x1, waiting for transfers between devices, stage(): feat_left = lax.ppermute(flat_features[row_count - rim:], 'node', to_right)  7.76 us
    ppermute x1, waiting for transfers between devices, stage(): one_left = lax.ppermute(order_one[row_count - rim:], 'node', to_right)  5.18 us
    dot_general x10, matrix products, band_product(): jnp.einsum('bpq,bqf->bpf', bands[offset], extended[offset:offset + block_...  4.96 us
    ppermute x1, starting transfers between devices, stage(): feat_right = lax.ppermute(flat_features[:rim], 'node', to_left)  4.2 us
    ppermute x1, starting transfers between devices, stage(): one_left = lax.ppermute(order_one[row_count - rim:], 'node', to_right)  4.1 us
    ppermute x1, waiting for transfers between devices, stage(): feat_right = lax.ppermute(flat_features[:rim], 'node', to_left)  3.61 us
    ppermute x1, waiting for transfers between devices, stage(): one_right = lax.ppermute(order_one[:rim], 'node', to_left)  2.65 us
    ppermute x1, starting transfers between devices, stage(): feat_left = lax.ppermute(flat_features[row_count - rim:], 'node', to_right)  1.92 us
  transfers between devices with their start and end apart: 5, of which 4 were waited for; matrix products, arithmetic and copies ran while one was open for 16% of the time, Pallas kernels for 0%

profile of v1, /device:TPU:128, one launch (start us, length us, event | category | flops | bytes accessed | tf_op | source)
XLA Modules:
  0.0 51.4 jit_solution(2835843744474039861)
XLA Ops:
  0.0 1.9 %collective-permute-start = (bf16[1024,256]{1,0:T(8,128)(2,1)}, bf16[1024,256]{1,0:T(8,128)(2,1)S(1)}, u32[]{:S(2)}, u32[]{:S(2)}) collective-permute-start(bf16[1024,256]{1,0:T(8,128)(2,1)} %param.8), channel_id=1, source_target_pairs={{0,32},{32,64},{64,96},{96,128},{128,160},{160,192},{192,224},{1,3... | collective-permute-start | bytes 1572872 | tf_op jit(solution)/shard_map/ppermute | solution.py:13
  1.9 1.1 %fusion.128 = (bf16[1024,128]{1,0:T(8,128)(2,1)S(1)}, bf16[1024,128]{1,0:T(8,128)(2,1)S(1)}) fusion(bf16[1024,256]{1,0:T(8,128)(2,1)} %param.8), kind=kLoop, calls=%fused_computation.206 | loop fusion | bytes 1048576 | tf_op jit(solution)/shard_map/slice | solution.py:73
  3.1 0.8 %slice_bitcast_fusion.12 = (bf16[64,256]{1,0:T(8,128)(2,1)S(1)}, bf16[64,256]{1,0:T(8,128)(2,1)S(1)}, bf16[64,256]{1,0:T(8,128)(2,1)S(1)}) fusion(bf16[3,64,256]{2,1,0:T(8,128)(2,1)} %param.9), kind=kLoop, calls=%fused_computation.156 | loop fusion | bytes 196608 | tf_op jit(solution)/shard_map/jit(kron)/mul | solution.py:46
  4.9 1.2 %fusion.2 = (bf16[8,128,128]{2,1,0:T(8,128)(2,1)S(1)}, bf16[8,128,128]{2,1,0:T(8,128)(2,1)S(1)}, bf16[8,128,128]{2,1,0:T(8,128)(2,1)S(1)}, bf16[8,128,128]{2,1,0:T(8,128)(2,1)S(1)}, bf16[8,128,128]{2,1,0:T(8,128)(2,1)S(1)}) fusion(bf16[8,4,128,128]{3,2,1,0:T(8,128)(2,1)S(1)} %copy-done.1, f32[8,4]{1,0:T(8,128)S(1)} %copy.12, f32[8,4]{1,0:T(8,128)S(1)} %copy.11, ...), kind=kLoop, calls=%fused_computation.7 | loop fusion | flops 5111808 | bytes 2359936 | tf_op jit(solution)/shard_map/reduce_sum | solution.py:25
  6.2 0.4 fusion.58
  6.6 0.7 %fusion.34 = f32[1024,512]{1,0:T(8,128)S(1)} fusion(bf16[1024,128]{1,0:T(8,128)(2,1)S(1)} %get-tuple-element.27, bf16[1024,128]{1,0:T(8,128)(2,1)S(1)} %get-tuple-element.26, bf16[128,512]{1,0:T(8,128)(2,1)S(1)} %bitcast.132, bf16[128,512]{1,0:T(8,128)(2,1)S(1)} %fusion.88, bf16[128,512]{1,0:T(8,128)(2,1)S(1)} %bitcast.135), kind=kOutput, calls=%fused_computation.55 | convolution fusion | flops 406192128 | bytes 3014656 | tf_op jit(solution)/shard_map/dot_general | solution.py:87
  7.5 0.7 %broadcast_multiply_fusion = (bf16[4,128,4,128]{3,2,1,0:T(4,128)(2,1)S(1)}, bf16[4,128,4,128]{3,2,1,0:T(4,128)(2,1)S(1)}, bf16[4,128,4,128]{3,2,1,0:T(4,128)(2,1)S(1)}) fusion(bf16[128,128]{1,0:T(8,128)(2,1)S(1)} %get-tuple-element.50, bf16[4,4]{1,0:T(4,128)(2,1)S(1)} %fusion.103, bf16[128,128]{1,0:T(8,128)(2,1)S(1)} %get-tuple-element.52, ...), kind=kLoop, calls=%fused_computation.128 | loop fusion | flops 786432 | bytes 1671200 | tf_op jit(solution)/shard_map/jit(kron)/mul | solution.py:54
  8.3 0.4 add_add_fusion
  9.1 0.4 fusion.9
  11.4 4.2 %collective-permute-start.2 = (bf16[256,512]{1,0:T(8,128)(2,1)S(1)}, bf16[256,512]{1,0:T(8,128)(2,1)S(1)}, u32[]{:S(2)}, u32[]{:S(2)}) collective-permute-start(bf16[256,512]{1,0:T(8,128)(2,1)S(1)} %get-tuple-element.25), channel_id=1, source_target_pairs={{1,0},{2,1},{3,2},{4,3},{5,4},{6,5},{7,6},{8,7},{9,8},{10,9},{11,1... | collective-permute-start | bytes 786440 | tf_op jit(solution)/shard_map/ppermute | solution.py:148
  15.6 1.9 %collective-permute-start.1 = (bf16[256,512]{1,0:T(8,128)(2,1)S(1)}, bf16[256,512]{1,0:T(8,128)(2,1)S(1)}, u32[]{:S(2)}, u32[]{:S(2)}) collective-permute-start(bf16[256,512]{1,0:T(8,128)(2,1)S(1)} %get-tuple-element.24), channel_id=1, source_target_pairs={{0,1},{1,2},{2,3},{3,4},{4,5},{5,6},{6,7},{7,8},{8,9},{9,10},{10,1... | collective-permute-start | bytes 786440 | tf_op jit(solution)/shard_map/ppermute | solution.py:147
  17.5 0.4 fusion.91
  17.9 3.6 %collective-permute-done.2 = bf16[256,512]{1,0:T(8,128)(2,1)S(1)} collective-permute-done((bf16[256,512]{1,0:T(8,128)(2,1)S(1)}, bf16[256,512]{1,0:T(8,128)(2,1)S(1)}, u32[]{:S(2)}, u32[]{:S(2)}) %collective-permute-start.2) | collective-permute-done | bytes 262176 | tf_op jit(solution)/shard_map/ppermute | solution.py:148
  21.6 7.8 %collective-permute-done.1 = bf16[256,512]{1,0:T(8,128)(2,1)S(1)} collective-permute-done((bf16[256,512]{1,0:T(8,128)(2,1)S(1)}, bf16[256,512]{1,0:T(8,128)(2,1)S(1)}, u32[]{:S(2)}, u32[]{:S(2)}) %collective-permute-start.1) | collective-permute-done | bytes 262176 | tf_op jit(solution)/shard_map/ppermute | solution.py:147
  29.9 0.6 %fusion.5 = bf16[8,128,512]{2,1,0:T(8,128)(2,1)S(1)} fusion(f32[2,128,512]{2,1,0:T(8,128)S(1)} %get-tuple-element.23, f32[2,128,512]{2,1,0:T(8,128)S(1)} %get-tuple-element.22, f32[8,128,512]{2,1,0:T(8,128)S(1)} %fusion.12, f32[8,128,512]{2,1,0:T(8,128)S(1)} %fusion.91, f32[8,128,512]{2,1,0:T(8,128)S(1)} %fusion.10, f32[8,128,512]{2,1,0:T(8,128)S(1)} %fusion.11, ...), kind=kOutput, calls=%fused_computation.11 | convolution fusion | flops 138412032 | bytes 11796512 | tf_op jit(solution)/shard_map/bpq,bqf->bpf/dot_general | solution.py:33
  30.9 0.4 fusion.132
  31.8 1.9 %collective-permute-start.4 = (bf16[256,512]{1,0:T(8,128)(2,1)S(1)}, bf16[256,512]{1,0:T(8,128)(2,1)S(1)}, u32[]{:S(2)}, u32[]{:S(2)}) collective-permute-start(bf16[256,512]{1,0:T(8,128)(2,1)S(1)} %bitcast.140), channel_id=1, source_target_pairs={{1,0},{2,1},{3,2},{4,3},{5,4},{6,5},{7,6},{8,7},{9,8},{10,9},{11,1... | collective-permute-start | bytes 786440 | tf_op jit(solution)/shard_map/ppermute | solution.py:153
  33.7 4.1 %collective-permute-start.3 = (bf16[256,512]{1,0:T(8,128)(2,1)S(1)}, bf16[256,512]{1,0:T(8,128)(2,1)S(1)}, u32[]{:S(2)}, u32[]{:S(2)}) collective-permute-start(bf16[256,512]{1,0:T(8,128)(2,1)S(1)} %bitcast.139), channel_id=1, source_target_pairs={{0,1},{1,2},{2,3},{3,4},{4,5},{5,6},{6,7},{7,8},{8,9},{9,10},{10,1... | collective-permute-start | bytes 786440 | tf_op jit(solution)/shard_map/ppermute | solution.py:152
  38.0 1.3 %fusion.23 = f32[1024,512]{0,1:T(8,128)S(1)} fusion(bf16[1024,1024]{1,0:T(8,128)(2,1)S(1)} %constant_dynamic-update-slice_fusion, bf16[512,512]{1,0:T(8,128)(2,1)S(1)} %get-tuple-element.71, bf16[512,512]{1,0:T(8,128)(2,1)S(1)} %get-tuple-element.72), kind=kOutput, calls=%fused_computation.44 | convolution fusion | flops 1075838976 | bytes 5242880 | tf_op jit(solution)/shard_map/dot_general | solution.py:156
  39.7 2.6 %collective-permute-done.4 = bf16[256,512]{1,0:T(8,128)(2,1)S(1)} collective-permute-done((bf16[256,512]{1,0:T(8,128)(2,1)S(1)}, bf16[256,512]{1,0:T(8,128)(2,1)S(1)}, u32[]{:S(2)}, u32[]{:S(2)}) %collective-permute-start.4) | collective-permute-done | bytes 262176 | tf_op jit(solution)/shard_map/ppermute | solution.py:153
  42.4 5.2 %collective-permute-done.3 = bf16[256,512]{1,0:T(8,128)(2,1)S(1)} collective-permute-done((bf16[256,512]{1,0:T(8,128)(2,1)S(1)}, bf16[256,512]{1,0:T(8,128)(2,1)S(1)}, u32[]{:S(2)}, u32[]{:S(2)}) %collective-permute-start.3) | collective-permute-done | bytes 262176 | tf_op jit(solution)/shard_map/ppermute | solution.py:152
  48.1 1.1 %fusion.8 = bf16[8,128,512]{2,1,0:T(8,128)(2,1)S(1)} fusion(f32[2,128,512]{2,1,0:T(8,128)S(1)} %get-tuple-element.19, f32[2,128,512]{2,1,0:T(8,128)S(1)} %get-tuple-element.18, f32[8,128,512]{2,1,0:T(8,128)S(1)} %fusion.15, f32[8,128,512]{2,1,0:T(8,128)S(1)} %fusion.132, f32[8,128,512]{2,1,0:T(8,128)S(1)} %fusion.13, f32[8,128,512]{2,1,0:T(8,128)S(1)} %fusion.14, ...), kind=kOutput, calls=%fused_computation.15 | convolution fusion | flops 143654912 | bytes 12845088 | tf_op jit(solution)/shard_map/bpq,bqf->bpf/dot_general | solution.py:33
  49.2 0.8 %maximum_convert_fusion = bf16[1024,512]{0,1:T(8,128)(2,1)S(1)} fusion(f32[1024,512]{0,1:T(8,128)S(1)} %fusion.23, bf16[1024,512]{1,0:T(8,128)(2,1)S(1)} %bitcast.129, f32[512]{0:T(512)S(1)} %broadcast_bitcast_fusion, bf16[64,8,4,128]{3,2,1,0:T(4,128)(2,1)S(1)} %bitcast.131), kind=kOutput, calls=%fused_computation.18 | convolution fusion | flops 538968064 | bytes 4720640 | tf_op jit(solution)/shard_map/dot_general | solution.py:163
  50.0 1.4 %copy.15 = bf16[1024,4,128]{2,1,0:T(4,128)(2,1)} copy(bf16[1024,4,128]{0,2,1:T(8,128)(2,1)S(1)} %bitcast.130) | data formatting | bytes 2097152 | tf_op jit(solution)/shard_map/reshape | solution.py:164
  (68 shorter events, 5.9 us)
Async XLA Ops:
  0.0 4.4 %copy-start = (f32[256]{0:T(256)S(1)}, f32[256]{0:T(256)}, u32[]{:S(2)}) copy-start(f32[256]{0:T(256)} %param.10) | copy-start | bytes 3076
  0.0 4.4 %copy-start.5 = (s32[8]{0:T(128)S(1)}, s32[8]{0:T(128)}, u32[]{:S(2)}) copy-start(s32[8]{0:T(128)} %param.13) | copy-start | bytes 100
  0.0 4.5 %copy-start.3 = (s32[8,4]{0,1:T(4,128)S(1)}, s32[8,4]{0,1:T(4,128)}, u32[]{:S(2)}) copy-start(s32[8,4]{0,1:T(4,128)} %param.12) | copy-start | bytes 388
  0.0 4.9 %copy-start.1 = (bf16[8,4,128,128]{3,2,1,0:T(8,128)(2,1)S(1)}, bf16[8,4,128,128]{3,2,1,0:T(8,128)(2,1)}, u32[]{:S(2)}) copy-start(bf16[8,4,128,128]{3,2,1,0:T(8,128)(2,1)} %param.11) | copy-start | bytes 3145732
  0.0 8.3 %collective-permute-start = (bf16[1024,256]{1,0:T(8,128)(2,1)}, bf16[1024,256]{1,0:T(8,128)(2,1)S(1)}, u32[]{:S(2)}, u32[]{:S(2)}) collective-permute-start(bf16[1024,256]{1,0:T(8,128)(2,1)} %param.8), channel_id=1, source_target_pairs={{0,32},{32,64},{64,96},{96,128},{128,160},{160,192},{192,224},{1,3... | collective-permute-start | bytes 1572872 | tf_op jit(solution)/shard_map/ppermute | solution.py:13
  3.9 2.2 %copy-start.2 = (bf16[3,128,128]{2,1,0:T(8,128)(2,1)S(1)}, bf16[3,128,128]{2,1,0:T(8,128)(2,1)}, u32[]{:S(2)}) copy-start(bf16[3,128,128]{2,1,0:T(8,128)(2,1)} %param.14) | copy-start | bytes 294916
  4.3 1.9 %copy-start.4 = (f32[128]{0:T(128)S(1)}, f32[128]{0:T(128)}, u32[]{:S(2)}) copy-start(f32[128]{0:T(128)} %param.15) | copy-start | bytes 1540
  11.4 10.2 %collective-permute-start.2 = (bf16[256,512]{1,0:T(8,128)(2,1)S(1)}, bf16[256,512]{1,0:T(8,128)(2,1)S(1)}, u32[]{:S(2)}, u32[]{:S(2)}) collective-permute-start(bf16[256,512]{1,0:T(8,128)(2,1)S(1)} %get-tuple-element.25), channel_id=1, source_target_pairs={{1,0},{2,1},{3,2},{4,3},{5,4},{6,5},{7,6},{8,7},{9,8},{10,9},{11,1... | collective-permute-start | bytes 786440 | tf_op jit(solution)/shard_map/ppermute | solution.py:148
  15.6 13.7 %collective-permute-start.1 = (bf16[256,512]{1,0:T(8,128)(2,1)S(1)}, bf16[256,512]{1,0:T(8,128)(2,1)S(1)}, u32[]{:S(2)}, u32[]{:S(2)}) collective-permute-start(bf16[256,512]{1,0:T(8,128)(2,1)S(1)} %get-tuple-element.24), channel_id=1, source_target_pairs={{0,1},{1,2},{2,3},{3,4},{4,5},{5,6},{6,7},{7,8},{8,9},{9,10},{10,1... | collective-permute-start | bytes 786440 | tf_op jit(solution)/shard_map/ppermute | solution.py:147
  31.8 10.6 %collective-permute-start.4 = (bf16[256,512]{1,0:T(8,128)(2,1)S(1)}, bf16[256,512]{1,0:T(8,128)(2,1)S(1)}, u32[]{:S(2)}, u32[]{:S(2)}) collective-permute-start(bf16[256,512]{1,0:T(8,128)(2,1)S(1)} %bitcast.140), channel_id=1, source_target_pairs={{1,0},{2,1},{3,2},{4,3},{5,4},{6,5},{7,6},{8,7},{9,8},{10,9},{11,1... | collective-permute-start | bytes 786440 | tf_op jit(solution)/shard_map/ppermute | solution.py:153
  33.7 13.9 %collective-permute-start.3 = (bf16[256,512]{1,0:T(8,128)(2,1)S(1)}, bf16[256,512]{1,0:T(8,128)(2,1)S(1)}, u32[]{:S(2)}, u32[]{:S(2)}) collective-permute-start(bf16[256,512]{1,0:T(8,128)(2,1)S(1)} %bitcast.139), channel_id=1, source_target_pairs={{0,1},{1,2},{2,3},{3,4},{4,5},{5,6},{6,7},{7,8},{8,9},{9,10},{10,1... | collective-permute-start | bytes 786440 | tf_op jit(solution)/shard_map/ppermute | solution.py:152

commit v2 on v0

--- a/solution.py
+++ b/solution.py
@@ -40,16 +40,6 @@
     return total
 
 
-def pair_weight(conv_weight):
-    taps, chan_in, width = conv_weight.shape
-    eye = jnp.eye(2, dtype=conv_weight.dtype)
-    blocks = [jnp.kron(eye, conv_weight[k]) for k in range(taps)]
-    rows_in = jnp.arange(2 * chan_in, dtype=jnp.int32)[:, None]
-    cols_out = jnp.arange(2 * width, dtype=jnp.int32)[None, :]
-    place = (cols_out == rows_in // chan_in * width + rows_in % chan_in).astype(conv_weight.dtype)
-    return jnp.concatenate(blocks + [place], axis=0)
-
-
 def block_diag(weight, steps):
     return jnp.kron(jnp.eye(steps, dtype=weight.dtype), weight)
 
@@ -64,36 +54,32 @@
     block_count, block_rows = (tile_values.shape[0], tile_values.shape[2])
     feat_width = steps_dev * chan_out
     earlier = passed_along(inputs, "tm", 1)
-    wpair = pair_weight(conv_weight)
-    pair_w = 2 * chan_in
+    taps = conv_weight.shape[0]
+    s_idx = jnp.arange(steps_dev, dtype=jnp.int32)[:, None]
+    t_idx = jnp.arange(steps_dev, dtype=jnp.int32)[None, :]
+    w_cur = 0.0
+    w_prev = 0.0
+    for k in range(taps):
+        shift_cur = (s_idx == t_idx - 2 * k).astype(jnp.float32)
+        shift_prev = (s_idx - steps_dev == t_idx - 2 * k).astype(jnp.float32)
+        tap = conv_weight[k].astype(jnp.float32)
+        w_cur = w_cur + jnp.kron(shift_cur, tap)
+        w_prev = w_prev + jnp.kron(shift_prev, tap)
+    w_cur = w_cur.astype(jnp.bfloat16)
+    w_prev = w_prev.astype(jnp.bfloat16)
+    rows_in = jnp.arange(steps_dev * chan_in, dtype=jnp.int32)[:, None]
+    cols_out = jnp.arange(steps_dev * 2 * chan_out, dtype=jnp.int32)[None, :]
+    place = (cols_out == rows_in // chan_in * (2 * chan_out) + rows_in % chan_in).astype(jnp.bfloat16)
+    mixed = jnp.dot(inputs, w_cur, preferred_element_type=jnp.float32)
+    mixed = mixed + jnp.dot(inputs, place, preferred_element_type=jnp.float32)
+    mixed = mixed + jnp.dot(earlier, w_prev, preferred_element_type=jnp.float32)
+    mixed = mixed + jnp.tile(conv_bias, steps_dev)[None, :]
     pieces = []
-    for p in range(steps_dev // 2):
-        w_new, w_mid, w_old, w_place = (wpair[i * pair_w : (i + 1) * pair_w] for i in range(4))
-        newest = inputs[:, p * pair_w : (p + 1) * pair_w]
-        cur_l = [newest, newest]
-        cur_w = [w_new, w_place]
-        prev_l = []
-        prev_w = []
-        for lag, w in ((1, w_mid), (2, w_old)):
-            q = p - lag
-            if q >= 0:
-                cur_l.append(inputs[:, q * pair_w : (q + 1) * pair_w])
-                cur_w.append(w)
-            else:
-                q += steps_dev // 2
-                prev_l.append(earlier[:, q * pair_w : (q + 1) * pair_w])
-                prev_w.append(w)
-        mixed = jnp.dot(
-            jnp.concatenate(cur_l, axis=1), jnp.concatenate(cur_w, axis=0), preferred_element_type=jnp.float32
-        )
-        mixed = mixed + jnp.dot(
-            jnp.concatenate(prev_l, axis=1), jnp.concatenate(prev_w, axis=0), preferred_element_type=jnp.float32
-        )
-        for tt in range(2):
-            lo = tt * 2 * chan_out
-            linear = mixed[:, lo : lo + chan_out] + conv_bias[:chan_out]
-            gate = mixed[:, lo + chan_out : lo + 2 * chan_out] + conv_bias[chan_out:]
-            pieces.append(linear * jax.nn.sigmoid(gate))
+    for t in range(steps_dev):
+        lo = t * 2 * chan_out
+        linear = mixed[:, lo : lo + chan_out]
+        gate = mixed[:, lo + chan_out : lo + 2 * chan_out]
+        pieces.append(linear * jax.nn.sigmoid(gate))
     flat_features = jnp.concatenate(pieces, axis=1).astype(jnp.bfloat16)
     first_block = lax.axis_index("node") * block_count
     band_tiles = build_band(tile_values, tile_cols, tile_count, first_block)
@@ -173,4 +159,6 @@
         P(),
         P(),
     )
-    return jax.shard_map(stage, mesh=mesh, in_specs=placed, out_specs=P("node", "tm", None), check_vma=False)
+    return jax.shard_map(
+        stage, mesh=mesh, in_specs=placed, out_specs=P("node", "tm", None), check_vma=False
+    )

time: 52.5 us -> 56.5 us (1.076)
  the two profiles are of different devices: /device:TPU:128 before, /device:TPU:144 now
where the time goes in v2:
time: 56.5 us; the launch traced here: 56.1 us
  waiting for transfers between devices  19.3 us (34%)
  starting transfers between devices  14.2 us (25%)
  matrix products  13.2 us (23%)
  other arithmetic  4.75 us (8%)
  local copies, waits for them, and re-layouts  4.2 us (7%)
    ppermute x1, waiting for transfers between devices, stage(): feat_left = lax.ppermute(flat_features[row_count - rim:], 'node', to_right)  7.75 us
    ppermute x1, waiting for transfers between devices, stage(): one_left = lax.ppermute(order_one[row_count - rim:], 'node', to_right)  5.18 us
    dot_general x10, matrix products, band_product(): jnp.einsum('bpq,bqf->bpf', bands[offset], extended[offset:offset + block_...  5 us
    ppermute x1, starting transfers between devices, stage(): feat_right = lax.ppermute(flat_features[:rim], 'node', to_left)  4.21 us
    ppermute x1, starting transfers between devices, stage(): one_left = lax.ppermute(order_one[row_count - rim:], 'node', to_right)  4.1 us
    ppermute x1, waiting for transfers between devices, stage(): feat_right = lax.ppermute(flat_features[:rim], 'node', to_left)  4.08 us
    dot_general x1, matrix products, stage(): mixed = mixed + jnp.dot(inputs, place, preferred_element_type=jnp.float32)  3.93 us
    ppermute x1, waiting for transfers between devices, stage(): one_right = lax.ppermute(order_one[:rim], 'node', to_left)  2.29 us
  transfers between devices with their start and end apart: 5, of which 4 were waited for; matrix products, arithmetic and copies ran while one was open for 21% of the time, Pallas kernels for 0%

profile of v2, /device:TPU:144, one launch (start us, length us, event | category | flops | bytes accessed | tf_op | source)
XLA Modules:
  0.0 56.1 jit_solution(12343196191002170535)
XLA Ops:
  0.0 2.0 %collective-permute-start = (bf16[1024,256]{1,0:T(8,128)(2,1)}, bf16[1024,256]{1,0:T(8,128)(2,1)S(1)}, u32[]{:S(2)}, u32[]{:S(2)}) collective-permute-start(bf16[1024,256]{1,0:T(8,128)(2,1)} %param.8), channel_id=1, source_target_pairs={{0,32},{32,64},{64,96},{96,128},{128,160},{160,192},{192,224},{1,3... | collective-permute-start | bytes 1572872 | tf_op jit(solution)/shard_map/ppermute | solution.py:13
  2.1 0.8 %bitcast_convert_fusion.2 = (f32[64,256]{1,0:T(8,128)S(1)}, f32[64,256]{1,0:T(8,128)S(1)}, f32[64,256]{1,0:T(8,128)S(1)}) fusion(bf16[3,64,256]{2,1,0:T(8,128)(2,1)} %param.9), kind=kLoop, calls=%fused_computation.128 | loop fusion | flops 49152 | bytes 294912 | tf_op jit(solution)/shard_map/convert_element_type | solution.py:65
  3.0 3.9 %fusion.33 = f32[1024,1024]{0,1:T(8,128)} fusion(bf16[1024,256]{1,0:T(8,128)(2,1)} %param.8, s32[256]{0:T(256)S(1)} %fusion.86), kind=kOutput, calls=%fused_computation.56 | convolution fusion | flops 537133056 | bytes 4719616 | tf_op jit(solution)/shard_map/dot_general | solution.py:74
  7.4 1.2 %fusion.2 = (bf16[8,128,128]{2,1,0:T(8,128)(2,1)S(1)}, bf16[8,128,128]{2,1,0:T(8,128)(2,1)S(1)}, bf16[8,128,128]{2,1,0:T(8,128)(2,1)S(1)}, bf16[8,128,128]{2,1,0:T(8,128)(2,1)S(1)}, bf16[8,128,128]{2,1,0:T(8,128)(2,1)S(1)}) fusion(bf16[8,4,128,128]{3,2,1,0:T(8,128)(2,1)S(1)} %copy-done.3, f32[8,4]{1,0:T(8,128)S(1)} %copy.11, f32[8,4]{1,0:T(8,128)S(1)} %copy.10, ...), kind=kLoop, calls=%fused_computation.8 | loop fusion | flops 5111808 | bytes 2359936 | tf_op jit(solution)/shard_map/reduce_sum | solution.py:25
  8.7 0.7 %broadcast_multiply_fusion = (bf16[4,128,4,128]{3,2,1,0:T(4,128)(2,1)S(1)}, bf16[4,128,4,128]{3,2,1,0:T(4,128)(2,1)S(1)}, bf16[4,128,4,128]{3,2,1,0:T(4,128)(2,1)S(1)}) fusion(bf16[128,128]{1,0:T(8,128)(2,1)S(1)} %get-tuple-element.48, bf16[4,4]{1,0:T(4,128)(2,1)S(1)} %fusion.74, bf16[128,128]{1,0:T(8,128)(2,1)S(1)} %get-tuple-element.50, ...), kind=kLoop, calls=%fused_computation.107 | loop fusion | flops 786432 | bytes 1671200 | tf_op jit(solution)/shard_map/jit(kron)/mul | solution.py:44
  9.6 0.9 %add_convert_fusion = (bf16[4,64,4,256]{3,2,1,0:T(4,128)(2,1)S(1)}, bf16[4,64,4,256]{3,2,1,0:T(4,128)(2,1)S(1)}) fusion(f32[4,4]{1,0:T(4,128)S(1)} %get-tuple-element.65, f32[4,4]{1,0:T(4,128)S(1)} %get-tuple-element.63, f32[4,4]{1,0:T(4,128)S(1)} %get-tuple-element.62, f32[64,256]{1,0:T(8,128)S(1)} %get-tuple-element.52, ...), kind=kLoop, calls=%fused_computation.53 | loop fusion | flops 3145728 | bytes 1245568 | tf_op jit(solution)/shard_map/convert_element_type | solution.py:69
  10.8 0.7 %fusion.108 = f32[1024,1024]{0,1:T(8,128)S(1)} fusion(bf16[1024,256]{1,0:T(8,128)(2,1)S(1)} %copy-done.2, bf16[256,1024]{1,0:T(8,128)(2,1)S(1)} %bitcast.128), kind=kOutput, calls=%fused_computation.190 | convolution fusion | flops 536870912 | bytes 5242880 | tf_op jit(solution)/shard_map/dot_general | solution.py:73
  11.5 1.5 %copy-done.1 = f32[1024,1024]{0,1:T(8,128)S(1)} copy-done((f32[1024,1024]{0,1:T(8,128)S(1)}, f32[1024,1024]{0,1:T(8,128)}, u32[]{:S(2)}) %copy-start.1) | copy-done | bytes 4194328
  13.0 0.7 %add_bitcast_fusion = f32[1024,1024]{1,0:T(8,128)S(1)} fusion(f32[1024,1024]{0,1:T(8,128)S(1)} %fusion.108, f32[1024,1024]{0,1:T(8,128)S(1)} %copy-done.1, bf16[1024,256]{1,0:T(8,128)(2,1)S(1)} %collective-permute-done, bf16[256,1024]{1,0:T(8,128)(2,1)S(1)} %bitcast.127, f32[1024]{0:T(1024)S(1)} %bitcast.138), kind=kOutput, calls=%fused_computation.5 | convolution fusion | flops 540016640 | bytes 13635584 | tf_op jit(solution)/shard_map/dot_general | solution.py:75
  15.9 4.2 %collective-permute-start.2 = (bf16[256,512]{1,0:T(8,128)(2,1)S(1)}, bf16[256,512]{1,0:T(8,128)(2,1)S(1)}, u32[]{:S(2)}, u32[]{:S(2)}) collective-permute-start(bf16[256,512]{1,0:T(8,128)(2,1)S(1)} %get-tuple-element.25), channel_id=1, source_target_pairs={{1,0},{2,1},{3,2},{4,3},{5,4},{6,5},{7,6},{8,7},{9,8},{10,9},{11,1... | collective-permute-start | bytes 786440 | tf_op jit(solution)/shard_map/ppermute | solution.py:132
  20.1 1.9 %collective-permute-start.1 = (bf16[256,512]{1,0:T(8,128)(2,1)S(1)}, bf16[256,512]{1,0:T(8,128)(2,1)S(1)}, u32[]{:S(2)}, u32[]{:S(2)}) collective-permute-start(bf16[256,512]{1,0:T(8,128)(2,1)S(1)} %get-tuple-element.24), channel_id=1, source_target_pairs={{0,1},{1,2},{2,3},{3,4},{4,5},{5,6},{6,7},{7,8},{8,9},{9,10},{10,1... | collective-permute-start | bytes 786440 | tf_op jit(solution)/shard_map/ppermute | solution.py:131
  22.0 0.4 fusion.67
  22.4 4.1 %collective-permute-done.2 = bf16[256,512]{1,0:T(8,128)(2,1)S(1)} collective-permute-done((bf16[256,512]{1,0:T(8,128)(2,1)S(1)}, bf16[256,512]{1,0:T(8,128)(2,1)S(1)}, u32[]{:S(2)}, u32[]{:S(2)}) %collective-permute-start.2) | collective-permute-done | bytes 262176 | tf_op jit(solution)/shard_map/ppermute | solution.py:132
  26.6 7.8 %collective-permute-done.1 = bf16[256,512]{1,0:T(8,128)(2,1)S(1)} collective-permute-done((bf16[256,512]{1,0:T(8,128)(2,1)S(1)}, bf16[256,512]{1,0:T(8,128)(2,1)S(1)}, u32[]{:S(2)}, u32[]{:S(2)}) %collective-permute-start.1) | collective-permute-done | bytes 262176 | tf_op jit(solution)/shard_map/ppermute | solution.py:131
  34.9 0.7 %fusion.5 = bf16[8,128,512]{2,1,0:T(8,128)(2,1)S(1)} fusion(f32[2,128,512]{2,1,0:T(8,128)S(1)} %get-tuple-element.23, f32[2,128,512]{2,1,0:T(8,128)S(1)} %get-tuple-element.22, f32[8,128,512]{2,1,0:T(8,128)S(1)} %fusion.11, f32[8,128,512]{2,1,0:T(8,128)S(1)} %fusion.67, f32[8,128,512]{2,1,0:T(8,128)S(1)} %fusion.9, f32[8,128,512]{2,1,0:T(8,128)S(1)} %fusion.10, ...), kind=kOutput, calls=%fused_computation.12 | convolution fusion | flops 138412032 | bytes 11796512 | tf_op jit(solution)/shard_map/bpq,bqf->bpf/dot_general | solution.py:33
  36.0 0.4 fusion.109
  36.8 1.9 %collective-permute-start.4 = (bf16[256,512]{1,0:T(8,128)(2,1)S(1)}, bf16[256,512]{1,0:T(8,128)(2,1)S(1)}, u32[]{:S(2)}, u32[]{:S(2)}) collective-permute-start(bf16[256,512]{1,0:T(8,128)(2,1)S(1)} %bitcast.137), channel_id=1, source_target_pairs={{1,0},{2,1},{3,2},{4,3},{5,4},{6,5},{7,6},{8,7},{9,8},{10,9},{11,1... | collective-permute-start | bytes 786440 | tf_op jit(solution)/shard_map/ppermute | solution.py:137
  38.7 4.1 %collective-permute-start.3 = (bf16[256,512]{1,0:T(8,128)(2,1)S(1)}, bf16[256,512]{1,0:T(8,128)(2,1)S(1)}, u32[]{:S(2)}, u32[]{:S(2)}) collective-permute-start(bf16[256,512]{1,0:T(8,128)(2,1)S(1)} %bitcast.136), channel_id=1, source_target_pairs={{0,1},{1,2},{2,3},{3,4},{4,5},{5,6},{6,7},{7,8},{8,9},{9,10},{10,1... | collective-permute-start | bytes 786440 | tf_op jit(solution)/shard_map/ppermute | solution.py:136
  43.0 1.3 %fusion.22 = f32[1024,512]{0,1:T(8,128)S(1)} fusion(bf16[1024,1024]{1,0:T(8,128)(2,1)S(1)} %constant_dynamic-update-slice_fusion, bf16[512,512]{1,0:T(8,128)(2,1)S(1)} %get-tuple-element.71, bf16[512,512]{1,0:T(8,128)(2,1)S(1)} %get-tuple-element.72), kind=kOutput, calls=%fused_computation.42 | convolution fusion | flops 1075838976 | bytes 5242880 | tf_op jit(solution)/shard_map/dot_general | solution.py:140
  44.7 2.3 %collective-permute-done.4 = bf16[256,512]{1,0:T(8,128)(2,1)S(1)} collective-permute-done((bf16[256,512]{1,0:T(8,128)(2,1)S(1)}, bf16[256,512]{1,0:T(8,128)(2,1)S(1)}, u32[]{:S(2)}, u32[]{:S(2)}) %collective-permute-start.4) | collective-permute-done | bytes 262176 | tf_op jit(solution)/shard_map/ppermute | solution.py:137
  47.1 5.2 %collective-permute-done.3 = bf16[256,512]{1,0:T(8,128)(2,1)S(1)} collective-permute-done((bf16[256,512]{1,0:T(8,128)(2,1)S(1)}, bf16[256,512]{1,0:T(8,128)(2,1)S(1)}, u32[]{:S(2)}, u32[]{:S(2)}) %collective-permute-start.3) | collective-permute-done | bytes 262176 | tf_op jit(solution)/shard_map/ppermute | solution.py:136
  52.8 1.1 %fusion.8 = bf16[8,128,512]{2,1,0:T(8,128)(2,1)S(1)} fusion(f32[2,128,512]{2,1,0:T(8,128)S(1)} %get-tuple-element.19, f32[2,128,512]{2,1,0:T(8,128)S(1)} %get-tuple-element.18, f32[8,128,512]{2,1,0:T(8,128)S(1)} %fusion.14, f32[8,128,512]{2,1,0:T(8,128)S(1)} %fusion.109, f32[8,128,512]{2,1,0:T(8,128)S(1)} %fusion.12, f32[8,128,512]{2,1,0:T(8,128)S(1)} %fusion.13, ...), kind=kOutput, calls=%fused_computation.16 | convolution fusion | flops 143654912 | bytes 12845088 | tf_op jit(solution)/shard_map/bpq,bqf->bpf/dot_general | solution.py:33
  53.9 0.8 %maximum_convert_fusion = bf16[1024,512]{0,1:T(8,128)(2,1)S(1)} fusion(f32[1024,512]{0,1:T(8,128)S(1)} %fusion.22, bf16[1024,512]{1,0:T(8,128)(2,1)S(1)} %bitcast.133, f32[512]{0:T(512)S(1)} %broadcast_bitcast_fusion.1, bf16[64,8,4,128]{3,2,1,0:T(4,128)(2,1)S(1)} %bitcast.135), kind=kOutput, calls=%fused_computation.17 | convolution fusion | flops 538968064 | bytes 4720640 | tf_op jit(solution)/shard_map/dot_general | solution.py:147
  54.7 1.4 %copy.14 = bf16[1024,4,128]{2,1,0:T(4,128)(2,1)} copy(bf16[1024,4,128]{0,2,1:T(8,128)(2,1)S(1)} %bitcast.134) | data formatting | bytes 2097152 | tf_op jit(solution)/shard_map/reshape | solution.py:148
  (70 shorter events, 5.6 us)
Async XLA Ops:
  0.0 6.9 %copy-start = (f32[256]{0:T(256)S(1)}, f32[256]{0:T(256)}, u32[]{:S(2)}) copy-start(f32[256]{0:T(256)} %param.10) | copy-start | bytes 3076
  0.0 11.5 %collective-permute-start = (bf16[1024,256]{1,0:T(8,128)(2,1)}, bf16[1024,256]{1,0:T(8,128)(2,1)S(1)}, u32[]{:S(2)}, u32[]{:S(2)}) collective-permute-start(bf16[1024,256]{1,0:T(8,128)(2,1)} %param.8), channel_id=1, source_target_pairs={{0,32},{32,64},{64,96},{96,128},{128,160},{160,192},{192,224},{1,3... | collective-permute-start | bytes 1572872 | tf_op jit(solution)/shard_map/ppermute | solution.py:13
  2.9 4.0 %copy-start.5 = (s32[8,4]{0,1:T(4,128)S(1)}, s32[8,4]{0,1:T(4,128)}, u32[]{:S(2)}) copy-start(s32[8,4]{0,1:T(4,128)} %param.12) | copy-start | bytes 388
  2.9 4.0 %copy-start.7 = (s32[8]{0:T(128)S(1)}, s32[8]{0:T(128)}, u32[]{:S(2)}) copy-start(s32[8]{0:T(128)} %param.13) | copy-start | bytes 100
  2.9 4.4 %copy-start.3 = (bf16[8,4,128,128]{3,2,1,0:T(8,128)(2,1)S(1)}, bf16[8,4,128,128]{3,2,1,0:T(8,128)(2,1)}, u32[]{:S(2)}) copy-start(bf16[8,4,128,128]{3,2,1,0:T(8,128)(2,1)} %param.11) | copy-start | bytes 3145732
  6.9 1.7 %copy-start.4 = (bf16[3,128,128]{2,1,0:T(8,128)(2,1)S(1)}, bf16[3,128,128]{2,1,0:T(8,128)(2,1)}, u32[]{:S(2)}) copy-start(bf16[3,128,128]{2,1,0:T(8,128)(2,1)} %param.14) | copy-start | bytes 294916
  6.9 1.7 %copy-start.6 = (f32[128]{0:T(128)S(1)}, f32[128]{0:T(128)}, u32[]{:S(2)}) copy-start(f32[128]{0:T(128)} %param.15) | copy-start | bytes 1540
  9.5 1.2 %copy-start.2 = (bf16[1024,256]{1,0:T(8,128)(2,1)S(1)}, bf16[1024,256]{1,0:T(8,128)(2,1)}, u32[]{:S(2)}) copy-start(bf16[1024,256]{1,0:T(8,128)(2,1)} %param.8) | copy-start | bytes 1572868
  10.8 2.2 %copy-start.1 = (f32[1024,1024]{0,1:T(8,128)S(1)}, f32[1024,1024]{0,1:T(8,128)}, u32[]{:S(2)}) copy-start(f32[1024,1024]{0,1:T(8,128)} %fusion.33) | copy-start | bytes 12582916
  15.9 10.7 %collective-permute-start.2 = (bf16[256,512]{1,0:T(8,128)(2,1)S(1)}, bf16[256,512]{1,0:T(8,128)(2,1)S(1)}, u32[]{:S(2)}, u32[]{:S(2)}) collective-permute-start(bf16[256,512]{1,0:T(8,128)(2,1)S(1)} %get-tuple-element.25), channel_id=1, source_target_pairs={{1,0},{2,1},{3,2},{4,3},{5,4},{6,5},{7,6},{8,7},{9,8},{10,9},{11,1... | collective-permute-start | bytes 786440 | tf_op jit(solution)/shard_map/ppermute | solution.py:132
  20.1 14.3 %collective-permute-start.1 = (bf16[256,512]{1,0:T(8,128)(2,1)S(1)}, bf16[256,512]{1,0:T(8,128)(2,1)S(1)}, u32[]{:S(2)}, u32[]{:S(2)}) collective-permute-start(bf16[256,512]{1,0:T(8,128)(2,1)S(1)} %get-tuple-element.24), channel_id=1, source_target_pairs={{0,1},{1,2},{2,3},{3,4},{4,5},{5,6},{6,7},{7,8},{8,9},{9,10},{10,1... | collective-permute-start | bytes 786440 | tf_op jit(solution)/shard_map/ppermute | solution.py:131
  36.8 10.2 %collective-permute-start.4 = (bf16[256,512]{1,0:T(8,128)(2,1)S(1)}, bf16[256,512]{1,0:T(8,128)(2,1)S(1)}, u32[]{:S(2)}, u32[]{:S(2)}) collective-permute-start(bf16[256,512]{1,0:T(8,128)(2,1)S(1)} %bitcast.137), channel_id=1, source_target_pairs={{1,0},{2,1},{3,2},{4,3},{5,4},{6,5},{7,6},{8,7},{9,8},{10,9},{11,1... | collective-permute-start | bytes 786440 | tf_op jit(solution)/shard_map/ppermute | solution.py:137
  38.7 13.5 %collective-permute-start.3 = (bf16[256,512]{1,0:T(8,128)(2,1)S(1)}, bf16[256,512]{1,0:T(8,128)(2,1)S(1)}, u32[]{:S(2)}, u32[]{:S(2)}) collective-permute-start(bf16[256,512]{1,0:T(8,128)(2,1)S(1)} %bitcast.136), channel_id=1, source_target_pairs={{0,1},{1,2},{2,3},{3,4},{4,5},{5,6},{6,7},{7,8},{8,9},{9,10},{10,1... | collective-permute-start | bytes 786440 | tf_op jit(solution)/shard_map/ppermute | solution.py:136

commit v3 on v1

--- a/solution.py
+++ b/solution.py
@@ -152,7 +152,8 @@
     one_left = lax.ppermute(order_one[row_count - rim :], "node", to_right)
     one_right = lax.ppermute(order_one[:rim], "node", to_left)
     two_own = own_part(order_one)
-    kron = [block_diag(cheb_weight[k], steps_dev) for k in range(3)]
+    late_weight, _ = lax.optimization_barrier((cheb_weight, one_own))
+    kron = [block_diag(late_weight[k], steps_dev) for k in range(3)]
     early = jnp.dot(
         jnp.concatenate([flat_features, order_one], axis=1),
         jnp.concatenate(kron[:2], axis=0),
@@ -175,4 +176,6 @@
         P(),
         P(),
     )
-    return jax.shard_map(stage, mesh=mesh, in_specs=placed, out_specs=P("node", "tm", None), check_vma=False)
+    return jax.shard_map(
+        stage, mesh=mesh, in_specs=placed, out_specs=P("node", "tm", None), check_vma=False
+    )

time: 51.7 us -> 52.1 us (level)
  the two profiles are of different devices: /device:TPU:128 before, /device:TPU:136 now
where the time goes in v3:
time: 52.1 us; the launch traced here: 51.8 us
  waiting for transfers between devices  18.9 us (36%)
  starting transfers between devices  14.2 us (27%)
  matrix products  9.73 us (19%)
  local copies, waits for them, and re-layouts  4.99 us (10%)
  other arithmetic  3.43 us (7%)
    ppermute x1, waiting for transfers between devices, stage(): feat_left = lax.ppermute(flat_features[row_count - rim:], 'node', to_right)  7.24 us
    ppermute x1, waiting for transfers between devices, stage(): one_left = lax.ppermute(order_one[row_count - rim:], 'node', to_right)  5.18 us
    dot_general x10, matrix products, band_product(): jnp.einsum('bpq,bqf->bpf', bands[offset], extended[offset:offset + block_...  4.94 us
    ppermute x1, starting transfers between devices, stage(): feat_right = lax.ppermute(flat_features[:rim], 'node', to_left)  4.22 us
    ppermute x1, starting transfers between devices, stage(): one_left = lax.ppermute(order_one[row_count - rim:], 'node', to_right)  4.1 us
    ppermute x1, waiting for transfers between devices, passed_along(): return lax.ppermute(value, axis, pairs)  3.31 us
    ppermute x1, waiting for transfers between devices, stage(): feat_right = lax.ppermute(flat_features[:rim], 'node', to_left)  2.83 us
    ppermute x1, starting transfers between devices, passed_along(): return lax.ppermute(value, axis, pairs)  2.05 us
  transfers between devices with their start and end apart: 5, of which 5 were waited for; matrix products, arithmetic and copies ran while one was open for 15% of the time, Pallas kernels for 0%

profile of v3, /device:TPU:136, one launch (start us, length us, event | category | flops | bytes accessed | tf_op | source)
XLA Modules:
  0.0 51.8 jit_solution(8343508624249786034)
XLA Ops:
  0.0 2.1 %collective-permute-start = (bf16[1024,256]{1,0:T(8,128)(2,1)}, bf16[1024,256]{1,0:T(8,128)(2,1)S(1)}, u32[]{:S(2)}, u32[]{:S(2)}) collective-permute-start(bf16[1024,256]{1,0:T(8,128)(2,1)} %param.8), channel_id=1, source_target_pairs={{0,32},{32,64},{64,96},{96,128},{128,160},{160,192},{192,224},{1,3... | collective-permute-start | bytes 1572872 | tf_op jit(solution)/shard_map/ppermute | solution.py:13
  2.1 1.1 %fusion.128 = (bf16[1024,128]{1,0:T(8,128)(2,1)S(1)}, bf16[1024,128]{1,0:T(8,128)(2,1)S(1)}) fusion(bf16[1024,256]{1,0:T(8,128)(2,1)} %param.8), kind=kLoop, calls=%fused_computation.207 | loop fusion | bytes 1048576 | tf_op jit(solution)/shard_map/slice | solution.py:73
  3.3 0.8 %slice_bitcast_fusion.12 = (bf16[64,256]{1,0:T(8,128)(2,1)S(1)}, bf16[64,256]{1,0:T(8,128)(2,1)S(1)}, bf16[64,256]{1,0:T(8,128)(2,1)S(1)}) fusion(bf16[3,64,256]{2,1,0:T(8,128)(2,1)} %param.9), kind=kLoop, calls=%fused_computation.157 | loop fusion | bytes 196608 | tf_op jit(solution)/shard_map/jit(kron)/mul | solution.py:46
  5.0 1.2 %fusion.4 = (bf16[8,128,128]{2,1,0:T(8,128)(2,1)S(1)}, bf16[8,128,128]{2,1,0:T(8,128)(2,1)S(1)}, bf16[8,128,128]{2,1,0:T(8,128)(2,1)S(1)}, bf16[8,128,128]{2,1,0:T(8,128)(2,1)S(1)}, bf16[8,128,128]{2,1,0:T(8,128)(2,1)S(1)}) fusion(bf16[8,4,128,128]{3,2,1,0:T(8,128)(2,1)S(1)} %copy-done.1, f32[8,4]{1,0:T(8,128)S(1)} %copy.14, f32[8,4]{1,0:T(8,128)S(1)} %copy.11, ...), kind=kLoop, calls=%fused_computation.9 | loop fusion | flops 5111808 | bytes 2359936 | tf_op jit(solution)/shard_map/reduce_sum | solution.py:25
  6.2 0.4 fusion.58
  6.8 0.7 %fusion.34 = f32[1024,512]{1,0:T(8,128)S(1)} fusion(bf16[1024,128]{1,0:T(8,128)(2,1)S(1)} %get-tuple-element.29, bf16[1024,128]{1,0:T(8,128)(2,1)S(1)} %get-tuple-element.28, bf16[128,512]{1,0:T(8,128)(2,1)S(1)} %bitcast.138, bf16[128,512]{1,0:T(8,128)(2,1)S(1)} %fusion.88, bf16[128,512]{1,0:T(8,128)(2,1)S(1)} %bitcast.135), kind=kOutput, calls=%fused_computation.56 | convolution fusion | flops 406192128 | bytes 3014656 | tf_op jit(solution)/shard_map/dot_general | solution.py:87
  7.6 3.3 %collective-permute-done = bf16[1024,256]{1,0:T(8,128)(2,1)S(1)} collective-permute-done((bf16[1024,256]{1,0:T(8,128)(2,1)}, bf16[1024,256]{1,0:T(8,128)(2,1)S(1)}, u32[]{:S(2)}, u32[]{:S(2)}) %collective-permute-start) | collective-permute-done | bytes 524320 | tf_op jit(solution)/shard_map/ppermute | solution.py:13
  10.9 0.4 add_add_fusion.1
  11.7 0.4 fusion.9
  13.9 4.2 %collective-permute-start.2 = (bf16[256,512]{1,0:T(8,128)(2,1)S(1)}, bf16[256,512]{1,0:T(8,128)(2,1)S(1)}, u32[]{:S(2)}, u32[]{:S(2)}) collective-permute-start(bf16[256,512]{1,0:T(8,128)(2,1)S(1)} %get-tuple-element.27), channel_id=1, source_target_pairs={{1,0},{2,1},{3,2},{4,3},{5,4},{6,5},{7,6},{8,7},{9,8},{10,9},{11,1... | collective-permute-start | bytes 786440 | tf_op jit(solution)/shard_map/ppermute | solution.py:148
  18.2 1.9 %collective-permute-start.1 = (bf16[256,512]{1,0:T(8,128)(2,1)S(1)}, bf16[256,512]{1,0:T(8,128)(2,1)S(1)}, u32[]{:S(2)}, u32[]{:S(2)}) collective-permute-start(bf16[256,512]{1,0:T(8,128)(2,1)S(1)} %get-tuple-element.26), channel_id=1, source_target_pairs={{0,1},{1,2},{2,3},{3,4},{4,5},{5,6},{6,7},{7,8},{8,9},{9,10},{10,1... | collective-permute-start | bytes 786440 | tf_op jit(solution)/shard_map/ppermute | solution.py:147
  20.5 2.8 %collective-permute-done.2 = bf16[256,512]{1,0:T(8,128)(2,1)S(1)} collective-permute-done((bf16[256,512]{1,0:T(8,128)(2,1)S(1)}, bf16[256,512]{1,0:T(8,128)(2,1)S(1)}, u32[]{:S(2)}, u32[]{:S(2)}) %collective-permute-start.2) | collective-permute-done | bytes 262176 | tf_op jit(solution)/shard_map/ppermute | solution.py:148
  23.4 7.2 %collective-permute-done.1 = bf16[256,512]{1,0:T(8,128)(2,1)S(1)} collective-permute-done((bf16[256,512]{1,0:T(8,128)(2,1)S(1)}, bf16[256,512]{1,0:T(8,128)(2,1)S(1)}, u32[]{:S(2)}, u32[]{:S(2)}) %collective-permute-start.1) | collective-permute-done | bytes 262176 | tf_op jit(solution)/shard_map/ppermute | solution.py:147
  31.2 0.6 %fusion.5 = bf16[8,128,512]{2,1,0:T(8,128)(2,1)S(1)} fusion(f32[2,128,512]{2,1,0:T(8,128)S(1)} %get-tuple-element.25, f32[2,128,512]{2,1,0:T(8,128)S(1)} %get-tuple-element.24, f32[8]{0:T(128)S(1)} %pad.29.clone, bf16[8,128,128]{2,1,0:T(8,128)(2,1)S(1)} %get-tuple-element.7, bf16[8,128,512]{2,1,0:T(8,128)(2,1)S(1)} %pad_maximum_fusion, ...), kind=kOutput, calls=%fused_computation.11 | convolution fusion | flops 138412032 | bytes 11796512 | tf_op jit(solution)/shard_map/bpq,bqf->bpf/dot_general | solution.py:33
  32.2 0.4 fusion.132
  33.0 0.5 copy-done.2
  33.5 0.7 %broadcast_multiply_fusion = (bf16[4,128,4,128]{3,2,1,0:T(4,128)(2,1)S(1)}, bf16[4,128,4,128]{3,2,1,0:T(4,128)(2,1)S(1)}, bf16[4,128,4,128]{3,2,1,0:T(4,128)(2,1)S(1)}) fusion(bf16[128,128]{1,0:T(8,128)(2,1)S(1)} %get-tuple-element.52, bf16[4,4]{1,0:T(4,128)(2,1)S(1)} %fusion.103, bf16[128,128]{1,0:T(8,128)(2,1)S(1)} %get-tuple-element.53, ...), kind=kLoop, calls=%fused_computation.129 | loop fusion | flops 786432 | bytes 1671200 | tf_op jit(solution)/shard_map/jit(kron)/mul | solution.py:54
  34.4 1.9 %collective-permute-start.4 = (bf16[256,512]{1,0:T(8,128)(2,1)S(1)}, bf16[256,512]{1,0:T(8,128)(2,1)S(1)}, u32[]{:S(2)}, u32[]{:S(2)}) collective-permute-start(bf16[256,512]{1,0:T(8,128)(2,1)S(1)} %bitcast.144), channel_id=1, source_target_pairs={{1,0},{2,1},{3,2},{4,3},{5,4},{6,5},{7,6},{8,7},{9,8},{10,9},{11,1... | collective-permute-start | bytes 786440 | tf_op jit(solution)/shard_map/ppermute | solution.py:153
  36.3 4.1 %collective-permute-start.3 = (bf16[256,512]{1,0:T(8,128)(2,1)S(1)}, bf16[256,512]{1,0:T(8,128)(2,1)S(1)}, u32[]{:S(2)}, u32[]{:S(2)}) collective-permute-start(bf16[256,512]{1,0:T(8,128)(2,1)S(1)} %bitcast.143), channel_id=1, source_target_pairs={{0,1},{1,2},{2,3},{3,4},{4,5},{5,6},{6,7},{7,8},{8,9},{9,10},{10,1... | collective-permute-start | bytes 786440 | tf_op jit(solution)/shard_map/ppermute | solution.py:152
  40.6 1.3 %fusion.23 = f32[1024,512]{0,1:T(8,128)S(1)} fusion(bf16[1024,1024]{1,0:T(8,128)(2,1)S(1)} %constant_dynamic-update-slice_fusion, bf16[512,512]{1,0:T(8,128)(2,1)S(1)} %bitcast.141, bf16[512,512]{1,0:T(8,128)(2,1)S(1)} %bitcast.142), kind=kOutput, calls=%fused_computation.45 | convolution fusion | flops 1075838976 | bytes 5242880 | tf_op jit(solution)/shard_map/dot_general | solution.py:157
  42.7 5.2 %collective-permute-done.3 = bf16[256,512]{1,0:T(8,128)(2,1)S(1)} collective-permute-done((bf16[256,512]{1,0:T(8,128)(2,1)S(1)}, bf16[256,512]{1,0:T(8,128)(2,1)S(1)}, u32[]{:S(2)}, u32[]{:S(2)}) %collective-permute-start.3) | collective-permute-done | bytes 262176 | tf_op jit(solution)/shard_map/ppermute | solution.py:152
  48.4 1.1 %fusion.8 = bf16[8,128,512]{2,1,0:T(8,128)(2,1)S(1)} fusion(f32[2,128,512]{2,1,0:T(8,128)S(1)} %get-tuple-element.21, f32[2,128,512]{2,1,0:T(8,128)S(1)} %get-tuple-element.20, f32[8,128,512]{2,1,0:T(8,128)S(1)} %fusion.15, f32[8,128,512]{2,1,0:T(8,128)S(1)} %fusion.132, f32[8,128,512]{2,1,0:T(8,128)S(1)} %fusion.13, f32[8,128,512]{2,1,0:T(8,128)S(1)} %fusion.14, ...), kind=kOutput, calls=%fused_computation.15 | convolution fusion | flops 143654912 | bytes 12845088 | tf_op jit(solution)/shard_map/bpq,bqf->bpf/dot_general | solution.py:33
  49.6 0.8 %maximum_convert_fusion = bf16[1024,512]{0,1:T(8,128)(2,1)S(1)} fusion(f32[1024,512]{0,1:T(8,128)S(1)} %fusion.23, bf16[1024,512]{1,0:T(8,128)(2,1)S(1)} %bitcast.131, f32[512]{0:T(512)S(1)} %broadcast_bitcast_fusion, bf16[64,8,4,128]{3,2,1,0:T(4,128)(2,1)S(1)} %bitcast.133), kind=kOutput, calls=%fused_computation.18 | convolution fusion | flops 538968064 | bytes 4720640 | tf_op jit(solution)/shard_map/dot_general | solution.py:164
  50.3 1.4 %copy.15 = bf16[1024,4,128]{2,1,0:T(4,128)(2,1)} copy(bf16[1024,4,128]{0,2,1:T(8,128)(2,1)S(1)} %bitcast.132) | data formatting | bytes 2097152 | tf_op jit(solution)/shard_map/reshape | solution.py:165
  (69 shorter events, 6.7 us)
Async XLA Ops:
  0.0 4.5 %copy-start = (f32[256]{0:T(256)S(1)}, f32[256]{0:T(256)}, u32[]{:S(2)}) copy-start(f32[256]{0:T(256)} %param.10) | copy-start | bytes 3076
  0.0 4.5 %copy-start.5 = (s32[8]{0:T(128)S(1)}, s32[8]{0:T(128)}, u32[]{:S(2)}) copy-start(s32[8]{0:T(128)} %param.13) | copy-start | bytes 100
  0.0 4.5 %copy-start.3 = (s32[8,4]{0,1:T(4,128)S(1)}, s32[8,4]{0,1:T(4,128)}, u32[]{:S(2)}) copy-start(s32[8,4]{0,1:T(4,128)} %param.12) | copy-start | bytes 388
  0.0 4.9 %copy-start.1 = (bf16[8,4,128,128]{3,2,1,0:T(8,128)(2,1)S(1)}, bf16[8,4,128,128]{3,2,1,0:T(8,128)(2,1)}, u32[]{:S(2)}) copy-start(bf16[8,4,128,128]{3,2,1,0:T(8,128)(2,1)} %param.11) | copy-start | bytes 3145732
  0.0 10.8 %collective-permute-start = (bf16[1024,256]{1,0:T(8,128)(2,1)}, bf16[1024,256]{1,0:T(8,128)(2,1)S(1)}, u32[]{:S(2)}, u32[]{:S(2)}) collective-permute-start(bf16[1024,256]{1,0:T(8,128)(2,1)} %param.8), channel_id=1, source_target_pairs={{0,32},{32,64},{64,96},{96,128},{128,160},{160,192},{192,224},{1,3... | collective-permute-start | bytes 1572872 | tf_op jit(solution)/shard_map/ppermute | solution.py:13
  6.7 0.8 %copy-start.4 = (f32[128]{0:T(128)S(1)}, f32[128]{0:T(128)}, u32[]{:S(2)}) copy-start(f32[128]{0:T(128)} %param.15) | copy-start | bytes 1540
  13.9 9.4 %collective-permute-start.2 = (bf16[256,512]{1,0:T(8,128)(2,1)S(1)}, bf16[256,512]{1,0:T(8,128)(2,1)S(1)}, u32[]{:S(2)}, u32[]{:S(2)}) collective-permute-start(bf16[256,512]{1,0:T(8,128)(2,1)S(1)} %get-tuple-element.27), channel_id=1, source_target_pairs={{1,0},{2,1},{3,2},{4,3},{5,4},{6,5},{7,6},{8,7},{9,8},{10,9},{11,1... | collective-permute-start | bytes 786440 | tf_op jit(solution)/shard_map/ppermute | solution.py:148
  18.2 12.5 %collective-permute-start.1 = (bf16[256,512]{1,0:T(8,128)(2,1)S(1)}, bf16[256,512]{1,0:T(8,128)(2,1)S(1)}, u32[]{:S(2)}, u32[]{:S(2)}) collective-permute-start(bf16[256,512]{1,0:T(8,128)(2,1)S(1)} %get-tuple-element.26), channel_id=1, source_target_pairs={{0,1},{1,2},{2,3},{3,4},{4,5},{5,6},{6,7},{7,8},{8,9},{9,10},{10,1... | collective-permute-start | bytes 786440 | tf_op jit(solution)/shard_map/ppermute | solution.py:147
  32.6 0.9 %copy-start.2 = (bf16[3,128,128]{2,1,0:T(8,128)(2,1)S(1)}, bf16[3,128,128]{2,1,0:T(8,128)(2,1)}, u32[]{:S(2)}) copy-start(bf16[3,128,128]{2,1,0:T(8,128)(2,1)} %param.14) | copy-start | bytes 294916
  34.4 8.3 %collective-permute-start.4 = (bf16[256,512]{1,0:T(8,128)(2,1)S(1)}, bf16[256,512]{1,0:T(8,128)(2,1)S(1)}, u32[]{:S(2)}, u32[]{:S(2)}) collective-permute-start(bf16[256,512]{1,0:T(8,128)(2,1)S(1)} %bitcast.144), channel_id=1, source_target_pairs={{1,0},{2,1},{3,2},{4,3},{5,4},{6,5},{7,6},{8,7},{9,8},{10,9},{11,1... | collective-permute-start | bytes 786440 | tf_op jit(solution)/shard_map/ppermute | solution.py:153
  36.3 11.6 %collective-permute-start.3 = (bf16[256,512]{1,0:T(8,128)(2,1)S(1)}, bf16[256,512]{1,0:T(8,128)(2,1)S(1)}, u32[]{:S(2)}, u32[]{:S(2)}) collective-permute-start(bf16[256,512]{1,0:T(8,128)(2,1)S(1)} %bitcast.143), channel_id=1, source_target_pairs={{0,1},{1,2},{2,3},{3,4},{4,5},{5,6},{6,7},{7,8},{8,9},{9,10},{10,1... | collective-permute-start | bytes 786440 | tf_op jit(solution)/shard_map/ppermute | solution.py:152
